TPU v7x, 512 devices: a whole 4x8x8 slice. The times are simulated.
512 devices in a mesh: ctx: 256 (over z, y, x_lo, core), kvh: 2 (over x_hi).
Axes of the slice: x: 4 (x_hi: 2, x_lo: 2; x = x_hi * 2 + x_lo), y: 8, z: 8, core: 2. Of those that a mesh axis runs over, the one named last changes fastest.
Arguments:
- queries: bfloat16 [65536, 64, 128], P('ctx', 'kvh'), may hold values from -110 to 110
- key_value: bfloat16 [2, 65536, 8, 128], P(None, 'ctx', 'kvh'), may hold values from -5 to 5
- span_table: int32 [512], replicated, may hold values from 0 to 511, as said below
Outputs:
- attended: bfloat16 [65536, 8192], P(('ctx', 'kvh'))
Inputs may be any that keep to these rules, and one draw needn't show every extreme that they name: `span_table`: entries 2 d and 2 d + 1 are the spans of ctx index d: the first below 256, the second 256 or above; every span of 0 to 511 appears exactly once.
All inputs are finite; a program needn't handle non-finite values.
Results may differ from a plain program's by a relative error of at most 0.0065.
Values may be sent and summed in bfloat16 or wider, within the bound.
No kernel may reach another device: no remote copies, remote signals or barrier semaphores. Data moves between devices by JAX's collectives and lax.ppermute only.
A program may use at most 64 MiB of HBM per device.

v0:
```python
import jax
import jax.numpy as jnp
from jax import lax
from jax.sharding import PartitionSpec as P

STEPS = 4


def passed_along(value, axis, steps):
    count = lax.axis_size(axis)
    pairs = [(source, (source + steps) % count) for source in range(count)]
    return lax.ppermute(value, axis, pairs)


def body(queries, key_value, span_table):
    rows = queries.shape[0]
    heads_here = queries.shape[1]
    head_size = queries.shape[2]
    kv_here = key_value.shape[2]
    group = heads_here // kv_here
    span = rows // 2
    scale = 1.0 / head_size**0.5
    cycle = lax.axis_size("ctx")
    myself = lax.axis_index("ctx")
    table = span_table.reshape(cycle, 2)
    offsets = jnp.arange(span, dtype=jnp.int32)

    def positions_of(device):
        pair = lax.dynamic_index_in_dim(table, device, 0, keepdims=False)
        return (pair[:, None] * span + offsets[None, :]).reshape(rows)

    query_pos = positions_of(myself)
    grouped = queries.reshape(rows, kv_here, group, head_size)

    def attend(carry, block, source):
        run_max, numer, denom = carry
        key_pos = positions_of(source)
        scores = (
            jnp.einsum("qghd,kgd->ghqk", grouped, block[0], preferred_element_type=jnp.float32)
            * scale
        )
        visible = (key_pos[None, :] <= query_pos[:, None])[None, None]
        masked = jnp.where(visible, scores, -jnp.inf)
        block_max = jnp.maximum(jnp.max(masked, axis=-1), jnp.float32(-1e30))
        weight = jnp.exp(masked - block_max[..., None])
        block_sum = jnp.sum(weight, axis=-1)
        block_out = jnp.einsum(
            "ghqk,kgd->ghqd",
            weight.astype(jnp.bfloat16),
            block[1],
            preferred_element_type=jnp.float32,
        )
        new_max = jnp.maximum(run_max, block_max)
        old_factor = jnp.exp(run_max - new_max)
        new_factor = jnp.exp(block_max - new_max)
        numer = numer * old_factor[..., None] + block_out * new_factor[..., None]
        denom = denom * old_factor + block_sum * new_factor
        return (new_max, numer, denom)

    start = (
        jnp.full((kv_here, group, rows), -1e30, jnp.float32),
        jnp.zeros((kv_here, group, rows, head_size), jnp.float32),
        jnp.zeros((kv_here, group, rows), jnp.float32),
    )
    carry = attend(start, key_value, myself)
    moving = key_value
    for distance in range(1, STEPS):
        moving = passed_along(moving, "ctx", 1)
        carry = attend(carry, moving, (myself - distance) % cycle)
    run_max, numer, denom = carry
    result = numer / denom[..., None]
    local_out = (
        jnp.transpose(result, (2, 0, 1, 3))
        .reshape(rows, heads_here * head_size)
        .astype(jnp.bfloat16)
    )
    return lax.all_to_all(local_out, "kvh", split_axis=0, concat_axis=1, tiled=True)


def solution(mesh):
    in_specs = (P("ctx", "kvh", None), P(None, "ctx", "kvh", None), P())
    out_specs = P(("ctx", "kvh"), None)
    return jax.shard_map(body, mesh=mesh, in_specs=in_specs, out_specs=out_specs, check_vma=False)
```

profile of v0, /device:TPU:4, one launch (start us, length us, event | category | flops | bytes accessed | tf_op | source)
XLA Modules:
  0.0 106.6 jit_solution(826526950033051445)
XLA Ops:
  0.0 0.0 copy-start
  0.0 1.3 %copy.27 = bf16[2,256,4,128]{3,1,2,0:T(8,128)(2,1)S(1)} copy(bf16[2,256,4,128]{3,2,1,0:T(4,128)(2,1)} %param.4) | data formatting | bytes 1048576 | tf_op args[1]
  1.3 1.9 %collective-permute-start = (bf16[2,256,4,128]{3,1,2,0:T(8,128)(2,1)S(1)}, bf16[2,256,4,128]{3,1,2,0:T(8,128)(2,1)S(1)}, u32[]{:S(2)}, u32[]{:S(2)}) collective-permute-start(bf16[2,256,4,128]{3,1,2,0:T(8,128)(2,1)S(1)} %copy.27), channel_id=1, source_target_pairs={{0,2},{2,4},{4,6},{6,8},{8,10},{10,12},{12,14},{14,16},{16,18},{18... | collective-permute-start | bytes 1572872 | tf_op jit(solution)/shard_map/ppermute | solution.py:12
  3.3 0.8 reshape.328
  4.1 0.1 add_bitcast_fusion
  4.2 0.1 add_bitcast_fusion.2
  4.3 0.2 broadcast_compare_fusion
  4.5 0.0 copy-done
  4.5 2.1 %fusion.8 = (f32[4,8,256]{2,1,0:T(8,128)S(1)}, f32[4,256,256,8]{2,1,3,0:T(8,128)S(1)}) fusion(pred[256,256]{0,1:T(8,128)(4,1)S(1)} %get-tuple-element.23, bf16[256,4,8,128]{3,2,1,0:T(8,128)(2,1)S(1)} %bitcast.239, bf16[2,256,4,128]{3,1,2,0:T(8,128)(2,1)S(1)} %copy.27), kind=kOutput, calls=%fused_computation.16 | convolution fusion | flops 543154176 | bytes 10846208 | tf_op jit(solution)/shard_map/qghd,kgd->ghqk/dot_general | solution.py:39
  6.7 2.4 %fusion.18 = f32[4,8,256,128]{3,2,1,0:T(8,128)S(1)} fusion(f32[4,256,256,8]{2,1,3,0:T(8,128)S(1)} %get-tuple-element.30, f32[4,8,256]{2,1,0:T(8,128)S(1)} %broadcast_maximum_fusion.3, pred[256,256]{0,1:T(8,128)(4,1)S(1)} %get-tuple-element.23, bf16[2,256,4,128]{3,1,2,0:T(8,128)(2,1)S(1)} %copy.27), kind=kOutput, calls=%fused_computation.23 | convolution fusion | flops 545259520 | bytes 12943360 | tf_op jit(solution)/shard_map/ghqk,kgd->ghqd/dot_general | solution.py:47
  9.0 1.8 %fusion = f32[4,8,256]{2,1,0:T(8,128)S(1)} fusion(f32[4,256,256,8]{2,1,3,0:T(8,128)S(1)} %get-tuple-element.30, f32[4,8,256]{2,1,0:T(8,128)S(1)} %broadcast_maximum_fusion.3, pred[256,256]{0,1:T(8,128)(4,1)S(1)} %get-tuple-element.23), kind=kLoop, calls=%fused_computation.8 | loop fusion | flops 8380416 | bytes 8519680 | tf_op jit(solution)/shard_map/reduce_sum | solution.py:46
  10.8 11.2 %collective-permute-done = bf16[2,256,4,128]{3,1,2,0:T(8,128)(2,1)S(1)} collective-permute-done((bf16[2,256,4,128]{3,1,2,0:T(8,128)(2,1)S(1)}, bf16[2,256,4,128]{3,1,2,0:T(8,128)(2,1)S(1)}, u32[]{:S(2)}, u32[]{:S(2)}) %collective-permute-start) | collective-permute-done | bytes 524320 | tf_op jit(solution)/shard_map/ppermute | solution.py:12
  22.1 2.1 %fusion.9 = (f32[4,8,256]{2,1,0:T(8,128)S(1)}, f32[4,256,256,8]{2,1,3,0:T(8,128)S(1)}) fusion(pred[256,256]{0,1:T(8,128)(4,1)S(1)} %get-tuple-element.24, bf16[256,4,8,128]{3,2,1,0:T(8,128)(2,1)S(1)} %bitcast.242, bf16[2,256,4,128]{3,1,2,0:T(8,128)(2,1)S(1)} %collective-permute-done), kind=kOutput, calls=%fused_computation.17 | convolution fusion | flops 543154176 | bytes 10846208 | tf_op jit(solution)/shard_map/qghd,kgd->ghqk/dot_general | solution.py:39
  24.2 2.1 %collective-permute-start.1 = (bf16[2,256,4,128]{3,1,2,0:T(8,128)(2,1)S(1)}, bf16[2,256,4,128]{3,1,2,0:T(8,128)(2,1)S(1)}, u32[]{:S(2)}, u32[]{:S(2)}) collective-permute-start(bf16[2,256,4,128]{3,1,2,0:T(8,128)(2,1)S(1)} %collective-permute-done), channel_id=1, source_target_pairs={{0,2},{2,4},{4,6},{6,8},{8,10},{10,12},{12,14},{14,16},{16,18},{18... | collective-permute-start | bytes 1572872 | tf_op jit(solution)/shard_map/ppermute | solution.py:12
  26.3 2.4 %fusion.16 = f32[4,8,256,128]{3,2,1,0:T(8,128)S(1)} fusion(f32[4,256,256,8]{2,1,3,0:T(8,128)S(1)} %get-tuple-element.28, f32[4,8,256]{2,1,0:T(8,128)S(1)} %broadcast_maximum_fusion.2, pred[256,256]{0,1:T(8,128)(4,1)S(1)} %get-tuple-element.24, bf16[2,256,4,128]{3,1,2,0:T(8,128)(2,1)S(1)} %collective-permute-done), kind=kOutput, calls=%fused_computation.22 | convolution fusion | flops 545259520 | bytes 12943360 | tf_op jit(solution)/shard_map/ghqk,kgd->ghqd/dot_general | solution.py:47
  28.7 1.8 %fusion.2 = f32[4,8,256]{2,1,0:T(8,128)S(1)} fusion(f32[4,256,256,8]{2,1,3,0:T(8,128)S(1)} %get-tuple-element.28, f32[4,8,256]{2,1,0:T(8,128)S(1)} %broadcast_maximum_fusion.2, pred[256,256]{0,1:T(8,128)(4,1)S(1)} %get-tuple-element.24), kind=kLoop, calls=%fused_computation.10 | loop fusion | flops 8380416 | bytes 8519680 | tf_op jit(solution)/shard_map/reduce_sum | solution.py:46
  30.5 8.4 %collective-permute-done.1 = bf16[2,256,4,128]{3,1,2,0:T(8,128)(2,1)S(1)} collective-permute-done((bf16[2,256,4,128]{3,1,2,0:T(8,128)(2,1)S(1)}, bf16[2,256,4,128]{3,1,2,0:T(8,128)(2,1)S(1)}, u32[]{:S(2)}, u32[]{:S(2)}) %collective-permute-start.1) | collective-permute-done | bytes 524320 | tf_op jit(solution)/shard_map/ppermute | solution.py:12
  38.9 2.1 %fusion.10 = (f32[4,8,256]{2,1,0:T(8,128)S(1)}, f32[4,256,256,8]{2,1,3,0:T(8,128)S(1)}) fusion(pred[256,256]{0,1:T(8,128)(4,1)S(1)} %get-tuple-element.22, bf16[256,4,8,128]{3,2,1,0:T(8,128)(2,1)S(1)} %bitcast.241, bf16[2,256,4,128]{3,1,2,0:T(8,128)(2,1)S(1)} %collective-permute-done.1), kind=kOutput, calls=%fused_computation.18 | convolution fusion | flops 543154176 | bytes 10846208 | tf_op jit(solution)/shard_map/qghd,kgd->ghqk/dot_general | solution.py:39
  41.1 2.1 %collective-permute-start.2 = (bf16[2,256,4,128]{3,1,2,0:T(8,128)(2,1)S(1)}, bf16[2,256,4,128]{3,1,2,0:T(8,128)(2,1)S(1)}, u32[]{:S(2)}, u32[]{:S(2)}) collective-permute-start(bf16[2,256,4,128]{3,1,2,0:T(8,128)(2,1)S(1)} %collective-permute-done.1), channel_id=1, source_target_pairs={{0,2},{2,4},{4,6},{6,8},{8,10},{10,12},{12,14},{14,16},{16,18},{18... | collective-permute-start | bytes 1572872 | tf_op jit(solution)/shard_map/ppermute | solution.py:12
  43.3 2.4 %fusion.14 = f32[4,8,256,128]{3,2,1,0:T(8,128)S(1)} fusion(f32[4,256,256,8]{2,1,3,0:T(8,128)S(1)} %get-tuple-element.26, f32[4,8,256]{2,1,0:T(8,128)S(1)} %broadcast_maximum_fusion.1, pred[256,256]{0,1:T(8,128)(4,1)S(1)} %get-tuple-element.22, bf16[2,256,4,128]{3,1,2,0:T(8,128)(2,1)S(1)} %collective-permute-done.1), kind=kOutput, calls=%fused_computation.21 | convolution fusion | flops 545259520 | bytes 12943360 | tf_op jit(solution)/shard_map/ghqk,kgd->ghqd/dot_general | solution.py:47
  45.6 1.8 %fusion.4 = f32[4,8,256]{2,1,0:T(8,128)S(1)} fusion(f32[4,256,256,8]{2,1,3,0:T(8,128)S(1)} %get-tuple-element.26, f32[4,8,256]{2,1,0:T(8,128)S(1)} %broadcast_maximum_fusion.1, pred[256,256]{0,1:T(8,128)(4,1)S(1)} %get-tuple-element.22), kind=kLoop, calls=%fused_computation.12 | loop fusion | flops 8380416 | bytes 8519680 | tf_op jit(solution)/shard_map/reduce_sum | solution.py:46
  47.4 8.4 %collective-permute-done.2 = bf16[2,256,4,128]{3,1,2,0:T(8,128)(2,1)S(1)} collective-permute-done((bf16[2,256,4,128]{3,1,2,0:T(8,128)(2,1)S(1)}, bf16[2,256,4,128]{3,1,2,0:T(8,128)(2,1)S(1)}, u32[]{:S(2)}, u32[]{:S(2)}) %collective-permute-start.2) | collective-permute-done | bytes 524320 | tf_op jit(solution)/shard_map/ppermute | solution.py:12
  55.8 2.1 %fusion.11 = (f32[4,8,256]{2,1,0:T(8,128)S(1)}, f32[4,256,256,8]{2,1,3,0:T(8,128)S(1)}) fusion(pred[256,256]{0,1:T(8,128)(4,1)S(1)} %get-tuple-element.21, bf16[256,4,8,128]{3,2,1,0:T(8,128)(2,1)S(1)} %bitcast.240, bf16[2,256,4,128]{3,1,2,0:T(8,128)(2,1)S(1)} %collective-permute-done.2), kind=kOutput, calls=%fused_computation.19 | convolution fusion | flops 543154176 | bytes 10846208 | tf_op jit(solution)/shard_map/qghd,kgd->ghqk/dot_general | solution.py:39
  58.0 1.8 %fusion.6 = f32[4,8,256]{2,1,0:T(8,128)S(1)} fusion(f32[4,256,256,8]{2,1,3,0:T(8,128)S(1)} %get-tuple-element.32, f32[4,8,256]{2,1,0:T(8,128)S(1)} %broadcast_maximum_fusion, pred[256,256]{0,1:T(8,128)(4,1)S(1)} %get-tuple-element.21), kind=kLoop, calls=%fused_computation.14 | loop fusion | flops 8380416 | bytes 8519680 | tf_op jit(solution)/shard_map/reduce_sum | solution.py:46
  59.8 0.1 fusion.57
  59.8 12.3 %fusion.22 = bf16[256,4,8,128]{3,0,2,1:T(8,128)(2,1)S(1)} fusion(f32[4,8,256,128]{3,2,1,0:T(8,128)S(1)} %fusion.14, f32[4,8,256,128]{3,2,1,0:T(8,128)S(1)} %fusion.16, f32[4,8,256,128]{3,2,1,0:T(8,128)S(1)} %fusion.18, f32[256,4,8]{0,2,1:T(8,128)S(1)} %get-tuple-element.7, f32[256,4,8]{0,2,1:T(8,128)S(1)} %get-tuple-element.10, ...), kind=kOutput, calls=%fused_computation.27 | convolution fusion | flops 558891008 | bytes 23724032 | tf_op jit(solution)/shard_map/ghqk,kgd->ghqd/dot_general | solution.py:47
  72.1 2.7 %copy.38 = bf16[256,4,8,128]{3,2,1,0:T(8,128)(2,1)} copy(bf16[256,4,8,128]{3,0,2,1:T(8,128)(2,1)S(1)} %fusion.22) | data formatting | bytes 4194304 | tf_op jit(solution)/shard_map/convert_element_type | solution.py:75
  74.8 4.2 %convert_element_type.24 = bf16[2,128,4096]{2,1,0:T(8,128)(2,1)} reshape(bf16[256,4,8,128]{3,2,1,0:T(8,128)(2,1)} %copy.38) | data formatting | bytes 4194304 | tf_op jit(solution)/shard_map/convert_element_type | solution.py:75
  79.0 19.5 %all_to_all.16 = bf16[2,128,4096]{2,1,0:T(8,128)(2,1)} all-to-all(bf16[2,128,4096]{2,1,0:T(8,128)(2,1)} %convert_element_type.24), channel_id=1, replica_groups=mesh['ctx'=256,'kvh'=2] {'kvh'}, dimensions={0} | all-to-all | bytes 4194304 | tf_op jit(solution)/shard_map/all_to_all | solution.py:77
  98.4 4.1 %copy.39 = bf16[128,2,4096]{0,2,1:T(8,128)(2,1)} copy(bf16[128,2,4096]{2,0,1:T(8,128)(2,1)} %bitcast.243) | data formatting | bytes 4194304 | tf_op jit(solution)/shard_map/all_to_all | solution.py:77
  102.5 4.1 %copy.40 = bf16[128,8192]{1,0:T(8,128)(2,1)} copy(bf16[128,8192]{0,1:T(8,128)(2,1)} %bitcast.244) | data formatting | bytes 4194304 | tf_op jit(solution)/shard_map/all_to_all | solution.py:77
  (6 shorter events, 0.1 us)
Async XLA Ops:
  0.0 4.5 %copy-start = (bf16[256,32,128]{2,1,0:T(8,128)(2,1)S(1)}, bf16[256,32,128]{2,1,0:T(8,128)(2,1)}, u32[]{:S(2)}) copy-start(bf16[256,32,128]{2,1,0:T(8,128)(2,1)} %param.3) | copy-start | bytes 6291460
  1.3 20.8 %collective-permute-start = (bf16[2,256,4,128]{3,1,2,0:T(8,128)(2,1)S(1)}, bf16[2,256,4,128]{3,1,2,0:T(8,128)(2,1)S(1)}, u32[]{:S(2)}, u32[]{:S(2)}) collective-permute-start(bf16[2,256,4,128]{3,1,2,0:T(8,128)(2,1)S(1)} %copy.27), channel_id=1, source_target_pairs={{0,2},{2,4},{4,6},{6,8},{8,10},{10,12},{12,14},{14,16},{16,18},{18... | collective-permute-start | bytes 1572872 | tf_op jit(solution)/shard_map/ppermute | solution.py:12
  24.2 14.7 %collective-permute-start.1 = (bf16[2,256,4,128]{3,1,2,0:T(8,128)(2,1)S(1)}, bf16[2,256,4,128]{3,1,2,0:T(8,128)(2,1)S(1)}, u32[]{:S(2)}, u32[]{:S(2)}) collective-permute-start(bf16[2,256,4,128]{3,1,2,0:T(8,128)(2,1)S(1)} %collective-permute-done), channel_id=1, source_target_pairs={{0,2},{2,4},{4,6},{6,8},{8,10},{10,12},{12,14},{14,16},{16,18},{18... | collective-permute-start | bytes 1572872 | tf_op jit(solution)/shard_map/ppermute | solution.py:12
  41.1 14.7 %collective-permute-start.2 = (bf16[2,256,4,128]{3,1,2,0:T(8,128)(2,1)S(1)}, bf16[2,256,4,128]{3,1,2,0:T(8,128)(2,1)S(1)}, u32[]{:S(2)}, u32[]{:S(2)}) collective-permute-start(bf16[2,256,4,128]{3,1,2,0:T(8,128)(2,1)S(1)} %collective-permute-done.1), channel_id=1, source_target_pairs={{0,2},{2,4},{4,6},{6,8},{8,10},{10,12},{12,14},{14,16},{16,18},{18... | collective-permute-start | bytes 1572872 | tf_op jit(solution)/shard_map/ppermute | solution.py:12
where the time goes:
time: 107 us
  waiting for transfers between devices  28.1 us (26%)
  matrix products  27.9 us (26%)
  blocking collectives  19.5 us (18%)
  local copies, waits for them, and re-layouts  17.1 us (16%)
  other arithmetic  7.65 us (7%)
  starting transfers between devices  6.16 us (6%)
    ppermute x3, waiting for transfers between devices, passed_along(): return lax.ppermute(value, axis, pairs)  28.1 us
    all_to_all x1, blocking collectives, body(): lax.all_to_all(local_out, 'kvh', split_axis=0, concat_axis=1, tiled=True)  19.5 us
    dot_general x4, matrix products, attend(): jnp.einsum('ghqk,kgd->ghqd', weight.astype(jnp.bfloat16), block[1], prefe...  19.3 us
    dot_general x4, matrix products, attend(): jnp.einsum('qghd,kgd->ghqk', grouped, block[0], preferred_element_type=jn...  8.5 us
    all_to_all x2, local copies, waits for them, and re-layouts, body(): lax.all_to_all(local_out, 'kvh', split_axis=0, concat_axis=1, tiled=True)  8.14 us
    reduce_sum x4, other arithmetic, attend(): block_sum = jnp.sum(weight, axis=-1)  7.15 us
    convert_element_type x2, local copies, waits for them, and re-layouts, body(): local_out = jnp.transpose(result, (2, 0, 1, 3)).reshape(rows, heads_here...  6.85 us
    ppermute x3, starting transfers between devices, passed_along(): return lax.ppermute(value, axis, pairs)  6.16 us
  transfers between devices with their start and end apart: 3, of which 3 were waited for; matrix products, arithmetic and copies ran while one was open for 15% of the time, Pallas kernels for 0%

commit v1 on v0

--- a/solution.py
+++ b/solution.py
@@ -74,7 +74,10 @@
         .reshape(rows, heads_here * head_size)
         .astype(jnp.bfloat16)
     )
-    return lax.all_to_all(local_out, "kvh", split_axis=0, concat_axis=1, tiled=True)
+    return jnp.concatenate(
+        lax.all_to_all(jnp.stack(jnp.split(local_out, lax.axis_size("kvh"), axis=0)), "kvh", 0, 0),
+        axis=1,
+    )
 
 
 def solution(mesh):

time: 107 us -> 90.2 us (0.84)
  local copies, waits for them, and re-layouts: 17.1 us -> 9.04 us
  matrix products: 27.9 us -> 21.7 us
  blocking collectives: 19.5 us -> 17.7 us
  waiting for transfers between devices: 28.1 us -> 27 us
    all_to_all x2 -> x0, local copies, waits for them, and re-layouts: 8.14 us -> none  [body(): lax.all_to_all(local_out, 'kvh', split_axis=0, concat_axis=1, tiled=True)]
    dot_general x4, matrix products: 19.3 us -> 12.3 us  [attend(): jnp.einsum('ghqk,kgd->ghqd', weight.astype(jnp.bfloat16), block[1], prefe...]
    convert_element_type x2 -> x0, local copies, waits for them, and re-layouts: 6.85 us -> none  [body(): local_out = jnp.transpose(result, (2, 0, 1, 3)).reshape(rows, heads_here...]
    reshape x0 -> x1, local copies, waits for them, and re-layouts: none -> 4.07 us  [body(): jnp.concatenate(lax.all_to_all(jnp.stack(jnp.split(local_out, lax.axis_si...]
    all_to_all x1, blocking collectives: 19.5 us -> 17.7 us  [body(): lax.all_to_all(jnp.stack(jnp.split(local_out, lax.axis_size('kvh'), axis=...]
    split x0 -> x1, local copies, waits for them, and re-layouts: none -> 1.68 us  [body(): jnp.split(local_out, lax.axis_size('kvh'), axis=0)]
    ppermute x3, waiting for transfers between devices: 28.1 us -> 27 us  [passed_along(): return lax.ppermute(value, axis, pairs)]
  transfers between devices with their start and end apart: 3 -> 3, of which waited for: 3 -> 3; matrix products, arithmetic and copies ran while one was open for 15% -> 19% of each run, Pallas kernels for 0% -> 0%
where the time goes in v1:
time: 90.2 us; the launch traced here: 89.8 us
  waiting for transfers between devices  27 us (30%)
  matrix products  21.7 us (24%)
  blocking collectives  17.7 us (20%)
  local copies, waits for them, and re-layouts  9.04 us (10%)
  other arithmetic  7.87 us (9%)
  starting transfers between devices  6.16 us (7%)
    ppermute x3, waiting for transfers between devices, passed_along(): return lax.ppermute(value, axis, pairs)  27 us
    all_to_all x1, blocking collectives, body(): lax.all_to_all(jnp.stack(jnp.split(local_out, lax.axis_size('kvh'), axis=...  17.7 us
    dot_general x4, matrix products, attend(): jnp.einsum('ghqk,kgd->ghqd', weight.astype(jnp.bfloat16), block[1], prefe...  12.3 us
    dot_general x4, matrix products, attend(): jnp.einsum('qghd,kgd->ghqk', grouped, block[0], preferred_element_type=jn...  9.49 us
    reduce_sum x4, other arithmetic, attend(): block_sum = jnp.sum(weight, axis=-1)  7.19 us
    ppermute x3, starting transfers between devices, passed_along(): return lax.ppermute(value, axis, pairs)  6.16 us
    reshape x1, local copies, waits for them, and re-layouts, body(): jnp.concatenate(lax.all_to_all(jnp.stack(jnp.split(local_out, lax.axis_si...  4.07 us
  transfers between devices with their start and end apart: 3, of which 3 were waited for; matrix products, arithmetic and copies ran while one was open for 19% of the time, Pallas kernels for 0%

profile of v1, /device:TPU:4, one launch (start us, length us, event | category | flops | bytes accessed | tf_op | source)
XLA Modules:
  0.0 89.8 jit_solution(726503232996676937)
XLA Ops:
  0.0 0.0 copy-start
  0.0 1.3 %copy.19 = bf16[2,256,4,128]{3,1,2,0:T(8,128)(2,1)S(1)} copy(bf16[2,256,4,128]{3,2,1,0:T(4,128)(2,1)} %param.4) | data formatting | bytes 1048576 | tf_op args[1]
  1.3 1.9 %collective-permute-start = (bf16[2,256,4,128]{3,1,2,0:T(8,128)(2,1)S(1)}, bf16[2,256,4,128]{3,1,2,0:T(8,128)(2,1)}, u32[]{:S(2)}, u32[]{:S(2)}) collective-permute-start(bf16[2,256,4,128]{3,1,2,0:T(8,128)(2,1)S(1)} %copy.19), channel_id=1, source_target_pairs={{0,2},{2,4},{4,6},{6,8},{8,10},{10,12},{12,14},{14,16},{16,18},{18... | collective-permute-start | bytes 1572872 | tf_op jit(solution)/shard_map/ppermute | solution.py:12
  3.3 1.0 %slice.27 = bf16[1,256,4,128]{3,2,1,0:T(4,128)(2,1)S(1)} slice(bf16[2,256,4,128]{3,2,1,0:T(4,128)(2,1)} %param.4), slice={[1:2], [0:256], [0:4], [0:128]} | slice | bytes 524288 | tf_op jit(solution)/shard_map/slice | solution.py:50
  4.3 0.8 reshape.334
  5.1 0.2 copy.53
  5.4 0.1 add_bitcast_fusion
  5.4 0.1 add_bitcast_fusion.2
  5.5 0.2 broadcast_compare_fusion
  5.7 0.0 copy-done
  5.7 2.1 %fusion.8 = (f32[4,8,256]{2,1,0:T(8,128)S(1)}, f32[4,256,256,8]{2,1,3,0:T(8,128)S(1)}) fusion(pred[256,256]{0,1:T(8,128)(4,1)S(1)} %get-tuple-element.25, bf16[256,4,8,128]{3,2,1,0:T(8,128)(2,1)S(1)} %bitcast.243, bf16[2,256,4,128]{3,1,2,0:T(8,128)(2,1)S(1)} %copy.19), kind=kOutput, calls=%fused_computation.16 | convolution fusion | flops 543154176 | bytes 10846208 | tf_op jit(solution)/shard_map/qghd,kgd->ghqk/dot_general | solution.py:39
  7.9 1.8 %fusion = f32[4,8,256]{2,1,0:T(8,128)S(1)} fusion(f32[4,256,256,8]{2,1,3,0:T(8,128)S(1)} %get-tuple-element.32, f32[4,8,256]{2,1,0:T(8,128)S(1)} %broadcast_maximum_fusion.3, pred[256,256]{0,1:T(8,128)(4,1)S(1)} %get-tuple-element.25), kind=kLoop, calls=%fused_computation.8 | loop fusion | flops 8380416 | bytes 8519680 | tf_op jit(solution)/shard_map/reduce_sum | solution.py:46
  9.7 2.2 %fusion.18 = f32[4,8,256,128]{2,3,1,0:T(8,128)S(1)} fusion(f32[4,256,256,8]{2,1,3,0:T(8,128)S(1)} %get-tuple-element.32, f32[4,8,256]{2,1,0:T(8,128)S(1)} %broadcast_maximum_fusion.3, pred[256,256]{0,1:T(8,128)(4,1)S(1)} %get-tuple-element.25, bf16[1,256,4,128]{1,3,2,0:T(8,128)(2,1)S(1)} %copy.53), kind=kOutput, calls=%fused_computation.23 | convolution fusion | flops 545259520 | bytes 12943360 | tf_op jit(solution)/shard_map/ghqk,kgd->ghqd/dot_general | solution.py:47
  11.9 10.2 %collective-permute-done = bf16[2,256,4,128]{3,1,2,0:T(8,128)(2,1)} collective-permute-done((bf16[2,256,4,128]{3,1,2,0:T(8,128)(2,1)S(1)}, bf16[2,256,4,128]{3,1,2,0:T(8,128)(2,1)}, u32[]{:S(2)}, u32[]{:S(2)}) %collective-permute-start) | collective-permute-done | bytes 524320 | tf_op jit(solution)/shard_map/ppermute | solution.py:12
  22.2 3.1 %fusion.9 = (f32[4,8,256]{2,1,0:T(8,128)S(1)}, f32[4,256,256,8]{2,1,3,0:T(8,128)S(1)}) fusion(pred[256,256]{0,1:T(8,128)(4,1)S(1)} %get-tuple-element.26, bf16[256,4,8,128]{3,2,1,0:T(8,128)(2,1)S(1)} %bitcast.246, bf16[2,256,4,128]{3,1,2,0:T(8,128)(2,1)} %collective-permute-done), kind=kOutput, calls=%fused_computation.17 | convolution fusion | flops 543154176 | bytes 10846208 | tf_op jit(solution)/shard_map/qghd,kgd->ghqk/dot_general | solution.py:39
  25.3 2.1 %collective-permute-start.1 = (bf16[2,256,4,128]{3,1,2,0:T(8,128)(2,1)}, bf16[2,256,4,128]{3,1,2,0:T(8,128)(2,1)S(1)}, u32[]{:S(2)}, u32[]{:S(2)}) collective-permute-start(bf16[2,256,4,128]{3,1,2,0:T(8,128)(2,1)} %collective-permute-done), channel_id=1, source_target_pairs={{0,2},{2,4},{4,6},{6,8},{8,10},{10,12},{12,14},{14,16},{16,18},{18... | collective-permute-start | bytes 1572872 | tf_op jit(solution)/shard_map/ppermute | solution.py:12
  27.4 3.0 %fusion.16 = f32[4,8,256,128]{2,3,1,0:T(8,128)S(1)} fusion(f32[4,256,256,8]{2,1,3,0:T(8,128)S(1)} %get-tuple-element.30, f32[4,8,256]{2,1,0:T(8,128)S(1)} %broadcast_maximum_fusion.2, pred[256,256]{0,1:T(8,128)(4,1)S(1)} %get-tuple-element.26, bf16[2,256,4,128]{3,1,2,0:T(8,128)(2,1)} %collective-permute-done), kind=kOutput, calls=%fused_computation.22 | convolution fusion | flops 545259520 | bytes 12943360 | tf_op jit(solution)/shard_map/ghqk,kgd->ghqd/dot_general | solution.py:47
  30.4 1.8 %fusion.2 = f32[4,8,256]{2,1,0:T(8,128)S(1)} fusion(f32[4,256,256,8]{2,1,3,0:T(8,128)S(1)} %get-tuple-element.30, f32[4,8,256]{2,1,0:T(8,128)S(1)} %broadcast_maximum_fusion.2, pred[256,256]{0,1:T(8,128)(4,1)S(1)} %get-tuple-element.26), kind=kLoop, calls=%fused_computation.10 | loop fusion | flops 8380416 | bytes 8519680 | tf_op jit(solution)/shard_map/reduce_sum | solution.py:46
  32.2 8.0 %collective-permute-done.1 = bf16[2,256,4,128]{3,1,2,0:T(8,128)(2,1)S(1)} collective-permute-done((bf16[2,256,4,128]{3,1,2,0:T(8,128)(2,1)}, bf16[2,256,4,128]{3,1,2,0:T(8,128)(2,1)S(1)}, u32[]{:S(2)}, u32[]{:S(2)}) %collective-permute-start.1) | collective-permute-done | bytes 524320 | tf_op jit(solution)/shard_map/ppermute | solution.py:12
  40.2 2.1 %fusion.10 = (f32[4,8,256]{2,1,0:T(8,128)S(1)}, f32[4,256,256,8]{2,1,3,0:T(8,128)S(1)}) fusion(pred[256,256]{0,1:T(8,128)(4,1)S(1)} %get-tuple-element.24, bf16[256,4,8,128]{3,2,1,0:T(8,128)(2,1)S(1)} %bitcast.245, bf16[2,256,4,128]{3,1,2,0:T(8,128)(2,1)S(1)} %collective-permute-done.1), kind=kOutput, calls=%fused_computation.18 | convolution fusion | flops 543154176 | bytes 10846208 | tf_op jit(solution)/shard_map/qghd,kgd->ghqk/dot_general | solution.py:39
  42.4 2.1 %collective-permute-start.2 = (bf16[2,256,4,128]{3,1,2,0:T(8,128)(2,1)S(1)}, bf16[2,256,4,128]{3,1,2,0:T(8,128)(2,1)S(1)}, u32[]{:S(2)}, u32[]{:S(2)}) collective-permute-start(bf16[2,256,4,128]{3,1,2,0:T(8,128)(2,1)S(1)} %collective-permute-done.1), channel_id=1, source_target_pairs={{0,2},{2,4},{4,6},{6,8},{8,10},{10,12},{12,14},{14,16},{16,18},{18... | collective-permute-start | bytes 1572872 | tf_op jit(solution)/shard_map/ppermute | solution.py:12
  44.5 2.0 %fusion.14 = f32[4,8,256,128]{2,3,1,0:T(8,128)S(1)} fusion(f32[4,256,256,8]{2,1,3,0:T(8,128)S(1)} %get-tuple-element.28, f32[4,8,256]{2,1,0:T(8,128)S(1)} %broadcast_maximum_fusion.1, pred[256,256]{0,1:T(8,128)(4,1)S(1)} %get-tuple-element.24, bf16[2,256,4,128]{3,1,2,0:T(8,128)(2,1)S(1)} %collective-permute-done.1), kind=kOutput, calls=%fused_computation.21 | convolution fusion | flops 545259520 | bytes 12943360 | tf_op jit(solution)/shard_map/ghqk,kgd->ghqd/dot_general | solution.py:47
  46.6 1.8 %fusion.4 = f32[4,8,256]{2,1,0:T(8,128)S(1)} fusion(f32[4,256,256,8]{2,1,3,0:T(8,128)S(1)} %get-tuple-element.28, f32[4,8,256]{2,1,0:T(8,128)S(1)} %broadcast_maximum_fusion.1, pred[256,256]{0,1:T(8,128)(4,1)S(1)} %get-tuple-element.24), kind=kLoop, calls=%fused_computation.12 | loop fusion | flops 8380416 | bytes 8519680 | tf_op jit(solution)/shard_map/reduce_sum | solution.py:46
  48.4 8.7 %collective-permute-done.2 = bf16[2,256,4,128]{3,1,2,0:T(8,128)(2,1)S(1)} collective-permute-done((bf16[2,256,4,128]{3,1,2,0:T(8,128)(2,1)S(1)}, bf16[2,256,4,128]{3,1,2,0:T(8,128)(2,1)S(1)}, u32[]{:S(2)}, u32[]{:S(2)}) %collective-permute-start.2) | collective-permute-done | bytes 524320 | tf_op jit(solution)/shard_map/ppermute | solution.py:12
  57.1 2.1 %fusion.11 = (f32[4,8,256]{2,1,0:T(8,128)S(1)}, f32[4,256,256,8]{2,1,3,0:T(8,128)S(1)}) fusion(pred[256,256]{0,1:T(8,128)(4,1)S(1)} %get-tuple-element.23, bf16[256,4,8,128]{3,2,1,0:T(8,128)(2,1)S(1)} %bitcast.244, bf16[2,256,4,128]{3,1,2,0:T(8,128)(2,1)S(1)} %collective-permute-done.2), kind=kOutput, calls=%fused_computation.19 | convolution fusion | flops 543154176 | bytes 10846208 | tf_op jit(solution)/shard_map/qghd,kgd->ghqk/dot_general | solution.py:39
  59.3 1.8 %fusion.6 = f32[4,8,256]{2,1,0:T(8,128)S(1)} fusion(f32[4,256,256,8]{2,1,3,0:T(8,128)S(1)} %get-tuple-element.34, f32[4,8,256]{2,1,0:T(8,128)S(1)} %broadcast_maximum_fusion, pred[256,256]{0,1:T(8,128)(4,1)S(1)} %get-tuple-element.23), kind=kLoop, calls=%fused_computation.14 | loop fusion | flops 8380416 | bytes 8519680 | tf_op jit(solution)/shard_map/reduce_sum | solution.py:46
  61.1 0.1 fusion.58
  61.1 5.0 %fusion.22 = bf16[256,4,8,128]{0,3,2,1:T(8,128)(2,1)} fusion(f32[4,8,256,128]{2,3,1,0:T(8,128)S(1)} %fusion.14, f32[4,8,256,128]{2,3,1,0:T(8,128)S(1)} %fusion.16, f32[4,8,256,128]{2,3,1,0:T(8,128)S(1)} %fusion.18, f32[256,4,8]{0,2,1:T(8,128)S(1)} %get-tuple-element.7, f32[256,4,8]{0,2,1:T(8,128)S(1)} %get-tuple-element.10, ...), kind=kOutput, calls=%fused_computation.27 | convolution fusion | flops 558891008 | bytes 23724032 | tf_op jit(solution)/shard_map/ghqk,kgd->ghqd/dot_general | solution.py:47
  66.2 1.7 %fusion.90 = (bf16[128,4,8,128]{0,3,2,1:T(8,128)(2,1)S(1)}, bf16[128,4,8,128]{0,3,2,1:T(8,128)(2,1)S(1)}) fusion(bf16[256,4,8,128]{0,3,2,1:T(8,128)(2,1)} %fusion.22), kind=kLoop, calls=%fused_computation.131 | loop fusion | bytes 4194304 | tf_op jit(solution)/shard_map/split | solution.py:78
  67.8 0.2 pad_maximum_fusion
  68.1 17.7 %all_to_all.5 = bf16[2,128,4096]{1,2,0:T(8,128)(2,1)} all-to-all(bf16[2,128,4096]{1,2,0:T(8,128)(2,1)S(1)} %pad_maximum_fusion), channel_id=1, replica_groups=mesh['ctx'=256,'kvh'=2] {'kvh'}, dimensions={0} | all-to-all | bytes 4194304 | tf_op jit(solution)/shard_map/all_to_all | solution.py:78
  85.7 4.1 %copy.52 = bf16[128,8192]{1,0:T(8,128)(2,1)} copy(bf16[128,8192]{0,1:T(8,128)(2,1)} %bitcast.247) | data formatting | bytes 4194304 | tf_op jit(solution)/shard_map/reshape | solution.py:77
  (6 shorter events, 0.1 us)
Async XLA Ops:
  0.0 5.7 %copy-start = (bf16[256,32,128]{2,1,0:T(8,128)(2,1)S(1)}, bf16[256,32,128]{2,1,0:T(8,128)(2,1)}, u32[]{:S(2)}) copy-start(bf16[256,32,128]{2,1,0:T(8,128)(2,1)} %param.3) | copy-start | bytes 6291460
  1.3 20.9 %collective-permute-start = (bf16[2,256,4,128]{3,1,2,0:T(8,128)(2,1)S(1)}, bf16[2,256,4,128]{3,1,2,0:T(8,128)(2,1)}, u32[]{:S(2)}, u32[]{:S(2)}) collective-permute-start(bf16[2,256,4,128]{3,1,2,0:T(8,128)(2,1)S(1)} %copy.19), channel_id=1, source_target_pairs={{0,2},{2,4},{4,6},{6,8},{8,10},{10,12},{12,14},{14,16},{16,18},{18... | collective-permute-start | bytes 1572872 | tf_op jit(solution)/shard_map/ppermute | solution.py:12
  25.3 14.9 %collective-permute-start.1 = (bf16[2,256,4,128]{3,1,2,0:T(8,128)(2,1)}, bf16[2,256,4,128]{3,1,2,0:T(8,128)(2,1)S(1)}, u32[]{:S(2)}, u32[]{:S(2)}) collective-permute-start(bf16[2,256,4,128]{3,1,2,0:T(8,128)(2,1)} %collective-permute-done), channel_id=1, source_target_pairs={{0,2},{2,4},{4,6},{6,8},{8,10},{10,12},{12,14},{14,16},{16,18},{18... | collective-permute-start | bytes 1572872 | tf_op jit(solution)/shard_map/ppermute | solution.py:12
  42.4 14.7 %collective-permute-start.2 = (bf16[2,256,4,128]{3,1,2,0:T(8,128)(2,1)S(1)}, bf16[2,256,4,128]{3,1,2,0:T(8,128)(2,1)S(1)}, u32[]{:S(2)}, u32[]{:S(2)}) collective-permute-start(bf16[2,256,4,128]{3,1,2,0:T(8,128)(2,1)S(1)} %collective-permute-done.1), channel_id=1, source_target_pairs={{0,2},{2,4},{4,6},{6,8},{8,10},{10,12},{12,14},{14,16},{16,18},{18... | collective-permute-start | bytes 1572872 | tf_op jit(solution)/shard_map/ppermute | solution.py:12
